TPU v7x, 128 devices: a whole 4x4x4 slice. The times are simulated.
128 devices in a mesh: grp: 4 (over y), tile: 32 (over x, z, core).
Axes of the slice: x: 4, y: 4, z: 4, core: 2. Of those that a mesh axis runs over, the one named last changes fastest.
Arguments:
- amp_tiles: bfloat16 [65536, 64, 64], P(('grp', 'tile')), may hold values from -6 to 6
- amp_row: int32 [65536], P(('grp', 'tile')), may hold values from 0 to 1024, as said below
- amp_col: int32 [65536], P(('grp', 'tile')), may hold values from 0 to 61
- cycle_panel: bfloat16 [3968, 3968], P('grp'), may hold values from -0.09375 to 0.09375
Outputs:
- residual: bfloat16 [65536, 64, 64], P(('grp', 'tile'))
Inputs may be any that keep to these rules, and one draw needn't show every extreme that they name: `amp_row`: tiles n of block k = n // 512 lie in group h = k // 32: their rows are h * 256 to (h + 1) * 256 - 1, or 1024 for an empty slot. No two non-empty tiles name the same row and column tile. Within one block of 512 tiles at most 16 name rows of one run r * 8 to (r + 1) * 8 - 1, and 16 is reached in every draw; in every group some run has all its 496 tiles present.
All inputs are finite; a program needn't handle non-finite values.
Results may differ from a plain program's by a relative error of at most 0.001.
Values may be sent and summed in bfloat16 or wider, within the bound.
No kernel may reach another device: no remote copies, remote signals or barrier semaphores. Data moves between devices by JAX's collectives and lax.ppermute only.
A program may use at most 192 MiB of HBM per device.

v0:
```python
import jax
import jax.numpy as jnp
from jax import lax
from jax.sharding import PartitionSpec as P

ROWT_DEV = 8


def body(amp_tiles, amp_row, amp_col, cycle_panel):
    parts = lax.axis_size("tile")
    count = amp_tiles.shape[0]
    capacity = count // parts
    edge = amp_tiles.shape[1]
    width = cycle_panel.shape[1]
    nvt = width // edge
    per_dest = ROWT_DEV * nvt
    group_rows = ROWT_DEV * parts
    first = lax.axis_index("grp") * group_rows
    local_row = amp_row - first
    live = local_row < group_rows
    target = jnp.where(live, local_row // ROWT_DEV, parts)
    onehot = (target[:, None] == jnp.arange(parts)[None, :]).astype(jnp.int32)
    rank = jnp.sum(jnp.cumsum(onehot, axis=0) * onehot, axis=1) - 1
    position = jnp.where(live, target * capacity + rank, parts * capacity)
    block_id = local_row % ROWT_DEV * nvt + amp_col
    flat = amp_tiles.reshape(count, edge * edge)
    send_tiles = (
        jnp.zeros((parts * capacity, edge * edge), jnp.bfloat16).at[position].set(flat, mode="drop")
    )
    send_ids = (
        jnp.full((parts * capacity,), per_dest, jnp.int32).at[position].set(block_id, mode="drop")
    )
    recv_tiles, recv_ids = (
        lax.all_to_all(send_tiles, "tile", split_axis=0, concat_axis=0, tiled=True),
        lax.all_to_all(send_ids, "tile", split_axis=0, concat_axis=0, tiled=True),
    )
    dense = (
        jnp.zeros((per_dest, edge * edge), jnp.bfloat16).at[recv_ids].set(recv_tiles, mode="drop")
    )
    dense = (
        dense.reshape(ROWT_DEV, nvt, edge, edge)
        .transpose(0, 2, 1, 3)
        .reshape(ROWT_DEV * edge, width)
    )
    cycle = jnp.dot(
        dense,
        lax.all_gather(cycle_panel, "grp", axis=0, tiled=True),
        preferred_element_type=jnp.float32,
    )
    cycle = cycle.astype(jnp.bfloat16)
    blocks_out = (
        cycle.reshape(ROWT_DEV, edge, nvt, edge)
        .transpose(0, 2, 1, 3)
        .reshape(per_dest, edge * edge)
    )
    answer = jnp.take(blocks_out, recv_ids, axis=0, mode="fill", fill_value=0)
    returned = lax.all_to_all(answer, "tile", split_axis=0, concat_axis=0, tiled=True)
    result = jnp.take(returned, position, axis=0, mode="fill", fill_value=0)
    return result.reshape(count, edge, edge)


def solution(mesh):
    in_specs = (
        P(("grp", "tile"), None, None),
        P(("grp", "tile")),
        P(("grp", "tile")),
        P("grp", None),
    )
    out_specs = P(("grp", "tile"), None, None)
    return jax.shard_map(body, mesh=mesh, in_specs=in_specs, out_specs=out_specs, check_vma=False)
```

profile of v0, /device:TPU:1, one launch (start us, length us, event | category | flops | bytes accessed | tf_op | source)
XLA Modules:
  0.0 457.8 jit_solution(15762808413656921646)
XLA Ops:
  7.3 1.2 reduce-window.6
  8.9 2.4 scatter_custom_fusion
  12.0 9.4 %all-to-all-start = ((s32[32,16,1]{1,2,0:T(1,128)}), s32[32,16,1]{1,2,0:T(1,128)S(1)}, u32[]{:S(2)}, u32[]{:S(2)}) async-start(s32[32,16,1]{1,2,0:T(1,128)} %bitcast.2), calls=%async_computation | async-start | bytes 32768 | tf_op jit(solution)/shard_map/all_to_all | solution.py:35
  21.4 6.9 %copy.20 = bf16[512,4096]{1,0:T(8,128)(2,1)} copy(bf16[512,4096]{0,1:T(8,128)(2,1)} %bitcast.43) | data formatting | bytes 8388608 | tf_op jit(solution)/shard_map/reshape | solution.py:26
  28.4 10.9 %scatter_custom_fusion.1 = bf16[512,4096]{1,0:T(8,128)(2,1)} fusion(s32[512]{0:T(512)S(1)} %get-tuple-element.6, bf16[512,4096]{1,0:T(8,128)(2,1)} %copy.20, bf16[]{:T(256)} %constant.84.clone.1), kind=kCustom, calls=%fused_computation.8 | custom fusion | bytes 4194816 | tf_op jit(solution)/shard_map/scatter | solution.py:28
  39.3 7.5 %all-to-all-start.1 = ((bf16[32,16,4096]{2,1,0:T(8,128)(2,1)}), bf16[32,16,4096]{2,1,0:T(8,128)(2,1)}, u32[]{:S(2)}, u32[]{:S(2)}) async-start(bf16[32,16,4096]{2,1,0:T(8,128)(2,1)} %bitcast.41), calls=%async_computation.1 | async-start | bytes 8388608 | tf_op jit(solution)/shard_map/all_to_all | solution.py:34
  48.1 50.8 %all-to-all-done.1 = bf16[32,16,4096]{2,1,0:T(8,128)(2,1)} async-done(((bf16[32,16,4096]{2,1,0:T(8,128)(2,1)}), bf16[32,16,4096]{2,1,0:T(8,128)(2,1)}, u32[]{:S(2)}, u32[]{:S(2)}) %all-to-all-start.1) | async-done | bytes 4194336 | tf_op jit(solution)/shard_map/all_to_all | solution.py:34
  98.9 10.3 %scatter_custom_fusion.2 = bf16[496,4096]{1,0:T(8,128)(2,1)} fusion(s32[512]{0:T(512)S(1)} %bitcast.47, bf16[512,4096]{1,0:T(8,128)(2,1)} %bitcast.7, bf16[]{:T(256)} %constant.84.clone.1), kind=kCustom, calls=%fused_computation.10 | custom fusion | bytes 4063744 | tf_op jit(solution)/shard_map/scatter | solution.py:38
  109.2 12.1 %reshape.91 = bf16[8,62,64,64]{3,2,1,0:T(8,128)(2,1)} reshape(bf16[496,4096]{1,0:T(8,128)(2,1)} %scatter_custom_fusion.2) | data formatting | bytes 8126464 | tf_op jit(solution)/shard_map/reshape | solution.py:41
  121.3 12.2 %copy.21 = bf16[8,64,62,64]{1,0,3,2:T(8,128)(2,1)} copy(bf16[8,64,62,64]{3,1,2,0:T(8,128)(2,1)} %bitcast.38) | data formatting | bytes 8126464 | tf_op jit(solution)/shard_map/transpose | solution.py:42
  133.5 11.5 %reshape.92 = bf16[512,3968]{0,1:T(8,128)(2,1)} reshape(bf16[8,64,62,64]{1,0,3,2:T(8,128)(2,1)} %copy.21) | data formatting | bytes 8126464 | tf_op jit(solution)/shard_map/reshape | solution.py:43
  145.0 143.5 %all-gather.2.cloned.1.call-done = bf16[3968,3968]{1,0:T(8,128)(2,1)} async-done(((bf16[992,3968]{1,0:T(8,128)(2,1)}), bf16[3968,3968]{1,0:T(8,128)(2,1)}) %all-gather.2.cloned.1.call-update) | async-done | bytes 31490064 | tf_op jit(solution)/shard_map/all_gather | solution.py:47
  288.4 23.6 %convolution_convert_fusion = bf16[512,3968]{1,0:T(8,128)(2,1)} fusion(bf16[512,3968]{0,1:T(8,128)(2,1)} %reshape.92, bf16[3968,3968]{1,0:T(8,128)(2,1)} %all-gather.2.cloned.1.call-done), kind=kOutput, calls=%fused_computation.5 | convolution fusion | flops 16124936192 | bytes 39616512 | tf_op jit(solution)/shard_map/dot_general | solution.py:45
  312.0 6.4 %copy.22 = bf16[512,3968]{0,1:T(8,128)(2,1)} copy(bf16[512,3968]{1,0:T(8,128)(2,1)} %convolution_convert_fusion) | data formatting | bytes 8126464 | tf_op jit(solution)/shard_map/convert_element_type | solution.py:50
  318.3 10.9 %reshape.93 = bf16[8,64,62,64]{1,0,3,2:T(8,128)(2,1)} reshape(bf16[512,3968]{0,1:T(8,128)(2,1)} %copy.22) | data formatting | bytes 8126464 | tf_op jit(solution)/shard_map/reshape | solution.py:52
  329.3 11.7 %copy.23 = bf16[8,62,64,64]{3,2,1,0:T(8,128)(2,1)} copy(bf16[8,62,64,64]{2,0,3,1:T(8,128)(2,1)} %bitcast.39) | data formatting | bytes 8126464 | tf_op jit(solution)/shard_map/transpose | solution.py:53
  341.0 11.7 %reshape.94 = bf16[496,4096]{1,0:T(8,128)(2,1)} reshape(bf16[8,62,64,64]{3,2,1,0:T(8,128)(2,1)} %copy.23) | data formatting | bytes 8126464 | tf_op jit(solution)/shard_map/reshape | solution.py:54
  352.7 11.3 %gather_fusion = bf16[512,4096]{1,0:T(8,128)(2,1)} fusion(bf16[496,4096]{1,0:T(8,128)(2,1)} %reshape.94, s32[1024]{0:T(1024)S(1)} %pad_clamp_fusion.1), kind=kCustom, calls=%fused_computation | custom fusion | bytes 8390656 | tf_op jit(solution)/shard_map/jit(_take)/gather | solution.py:56
  363.9 4.5 broadcast_select_fusion
  368.5 8.2 %all-to-all-start.2 = ((bf16[32,16,4096]{2,1,0:T(8,128)(2,1)}), bf16[32,16,4096]{2,1,0:T(8,128)(2,1)}, u32[]{:S(2)}, u32[]{:S(2)}) async-start(bf16[32,16,4096]{2,1,0:T(8,128)(2,1)} %broadcast_select_fusion), calls=%async_computation.2 | async-start | bytes 8388608 | tf_op jit(solution)/shard_map/all_to_all | solution.py:57
  376.6 52.1 %all-to-all-done.2 = bf16[32,16,4096]{2,1,0:T(8,128)(2,1)} async-done(((bf16[32,16,4096]{2,1,0:T(8,128)(2,1)}), bf16[32,16,4096]{2,1,0:T(8,128)(2,1)}, u32[]{:S(2)}, u32[]{:S(2)}) %all-to-all-start.2) | async-done | bytes 4194336 | tf_op jit(solution)/shard_map/all_to_all | solution.py:57
  428.8 11.3 %gather_fusion.1 = bf16[512,4096]{1,0:T(8,128)(2,1)} fusion(bf16[512,4096]{1,0:T(8,128)(2,1)} %bitcast.11, s32[1024]{0:T(1024)S(1)} %pad_clamp_fusion), kind=kCustom, calls=%fused_computation.1 | custom fusion | bytes 8390656 | tf_op jit(solution)/shard_map/jit(_take)/gather | solution.py:58
  440.1 6.5 %copy.24 = bf16[512,4096]{0,1:T(8,128)(2,1)} copy(bf16[512,4096]{1,0:T(8,128)(2,1)} %gather_fusion.1) | data formatting | bytes 8388608 | tf_op jit(solution)/shard_map/jit(_take)/gather | solution.py:58
  446.5 4.5 broadcast_select_fusion.1
  (22 shorter events, 3.1 us)
Async XLA Ops:
  6.5 0.7 copy-start
  6.5 0.7 copy-start.1
  6.5 281.9 %all-gather.2.cloned.1.call-start = ((), (), s32[]{:S(2)}) async-start(), calls=%async_computation.3 | async-start | bytes 39362560 | tf_op jit(solution)/shard_map/all_gather | solution.py:47
  12.0 27.3 %all-to-all-start = ((s32[32,16,1]{1,2,0:T(1,128)}), s32[32,16,1]{1,2,0:T(1,128)S(1)}, u32[]{:S(2)}, u32[]{:S(2)}) async-start(s32[32,16,1]{1,2,0:T(1,128)} %bitcast.2), calls=%async_computation | async-start | bytes 32768 | tf_op jit(solution)/shard_map/all_to_all | solution.py:35
  39.3 59.6 %all-to-all-start.1 = ((bf16[32,16,4096]{2,1,0:T(8,128)(2,1)}), bf16[32,16,4096]{2,1,0:T(8,128)(2,1)}, u32[]{:S(2)}, u32[]{:S(2)}) async-start(bf16[32,16,4096]{2,1,0:T(8,128)(2,1)} %bitcast.41), calls=%async_computation.1 | async-start | bytes 8388608 | tf_op jit(solution)/shard_map/all_to_all | solution.py:34
  368.5 60.3 %all-to-all-start.2 = ((bf16[32,16,4096]{2,1,0:T(8,128)(2,1)}), bf16[32,16,4096]{2,1,0:T(8,128)(2,1)}, u32[]{:S(2)}, u32[]{:S(2)}) async-start(bf16[32,16,4096]{2,1,0:T(8,128)(2,1)} %broadcast_select_fusion), calls=%async_computation.2 | async-start | bytes 8388608 | tf_op jit(solution)/shard_map/all_to_all | solution.py:57
Sparse Core Ops, SparseCore 0:
  9.0 279.3 all-gather.1
where the time goes:
time: 460 us; the launch traced here: 458 us
  waiting for transfers between devices  247 us (54%)
  local copies, waits for them, and re-layouts  138 us (30%)
  starting transfers between devices  25.1 us (5%)
  matrix products  23.6 us (5%)
  between operations  13.5 us (3%)
  other arithmetic  11.1 us (2%)
    all_gather x1, waiting for transfers between devices, body(): lax.all_gather(cycle_panel, 'grp', axis=0, tiled=True)  143 us
    all_to_all x1, waiting for transfers between devices, body(): lax.all_to_all(answer, 'tile', split_axis=0, concat_axis=0, tiled=True)  52.1 us
    all_to_all x1, waiting for transfers between devices, body(): lax.all_to_all(send_tiles, 'tile', split_axis=0, concat_axis=0, tiled=True)  50.8 us
    dot_general x1, matrix products, body(): jnp.dot(dense, lax.all_gather(cycle_panel, 'grp', axis=0, tiled=True), pr...  23.6 us
    gather x2, local copies, waits for them, and re-layouts, body(): result = jnp.take(returned, position, axis=0, mode='fill', fill_value=0)  17.8 us
    transpose x1, local copies, waits for them, and re-layouts, body(): dense = dense.reshape(ROWT_DEV, nvt, edge, edge).transpose(0, 2, 1, 3).re...  12.2 us
    reshape x1, local copies, waits for them, and re-layouts, body(): dense.reshape(ROWT_DEV, nvt, edge, edge).transpose(0, 2, 1, 3)  12.1 us
    transpose x1, local copies, waits for them, and re-layouts, body(): blocks_out = cycle.reshape(ROWT_DEV, edge, nvt, edge).transpose(0, 2, 1,...  11.7 us
  transfers between devices with their start and end apart: 4, of which 3 were waited for; matrix products, arithmetic and copies ran while one was open for 15% of the time, Pallas kernels for 0%

commit v1 on v0

--- a/solution.py
+++ b/solution.py
@@ -4,6 +4,19 @@
 from jax.sharding import PartitionSpec as P
 
 ROWT_DEV = 8
+
+
+def gather_around(value, axis, dim):
+    ways = lax.axis_size(axis)
+    up = [(d, (d + 1) % ways) for d in range(ways)]
+    down = [(d, (d - 1) % ways) for d in range(ways)]
+    earlier, later = ([value], [value])
+    for _ in range(ways // 2):
+        earlier.append(lax.ppermute(earlier[-1], axis, up))
+    for _ in range((ways - 1) // 2):
+        later.append(lax.ppermute(later[-1], axis, down))
+    line = jnp.concatenate([*earlier[::-1], *later[1:]], axis=dim)
+    return jnp.roll(line, (lax.axis_index(axis) - ways // 2) * value.shape[dim], axis=dim)
 
 
 def body(amp_tiles, amp_row, amp_col, cycle_panel):
@@ -42,11 +55,7 @@
         .transpose(0, 2, 1, 3)
         .reshape(ROWT_DEV * edge, width)
     )
-    cycle = jnp.dot(
-        dense,
-        lax.all_gather(cycle_panel, "grp", axis=0, tiled=True),
-        preferred_element_type=jnp.float32,
-    )
+    cycle = jnp.dot(dense, gather_around(cycle_panel, "grp", 0), preferred_element_type=jnp.float32)
     cycle = cycle.astype(jnp.bfloat16)
     blocks_out = (
         cycle.reshape(ROWT_DEV, edge, nvt, edge)

time: 460 us -> 568 us (1.23); the launches traced: 458 us -> 557 us
  waiting for transfers between devices: 247 us -> 303 us
  local copies, waits for them, and re-layouts: 138 us -> 186 us
  between operations: 13.5 us -> 0.35 us
  starting transfers between devices: 25.1 us -> 32.8 us
    ppermute x0 -> x3, waiting for transfers between devices: none -> 201 us  [the longest x2 201 us: gather_around(): earlier.append(lax.ppermute(earlier[-1], axis, up))]
    all_gather x1 -> x0, waiting for transfers between devices: 143 us -> none  [body(): lax.all_gather(cycle_panel, 'grp', axis=0, tiled=True)]
    unnamed x4 -> x13, local copies, waits for them, and re-layouts: 0.01 us -> 42.2 us
    concatenate x0 -> x1, local copies, waits for them, and re-layouts: none -> 6.99 us  [gather_around(): jnp.roll(line, (lax.axis_index(axis) - ways // 2) * value.shape[dim], axi...]
  transfers between devices with their start and end apart: 4 -> 6, of which waited for: 3 -> 4; matrix products, arithmetic and copies ran while one was open for 15% -> 16% of each run, Pallas kernels for 0% -> 0%
where the time goes in v1:
time: 568 us; the launch traced here: 557 us
  waiting for transfers between devices  303 us (53%)
  local copies, waits for them, and re-layouts  186 us (33%)
  starting transfers between devices  32.8 us (6%)
  matrix products  22.9 us (4%)
  other arithmetic  12.5 us (2%)
    ppermute x2, waiting for transfers between devices, gather_around(): earlier.append(lax.ppermute(earlier[-1], axis, up))  201 us
    all_to_all x1, waiting for transfers between devices, body(): lax.all_to_all(answer, 'tile', split_axis=0, concat_axis=0, tiled=True)  52.1 us
    all_to_all x1, waiting for transfers between devices, body(): lax.all_to_all(send_tiles, 'tile', split_axis=0, concat_axis=0, tiled=True)  50.6 us
    unnamed x13, local copies, waits for them, and re-layouts  42.2 us
    dot_general x1, matrix products, body(): jnp.dot(dense, gather_around(cycle_panel, 'grp', 0), preferred_element_ty...  22.9 us
    gather x2, local copies, waits for them, and re-layouts, body(): result = jnp.take(returned, position, axis=0, mode='fill', fill_value=0)  17.8 us
    reshape x1, local copies, waits for them, and re-layouts, body(): dense.reshape(ROWT_DEV, nvt, edge, edge).transpose(0, 2, 1, 3)  12.1 us
    transpose x1, local copies, waits for them, and re-layouts, body(): dense = dense.reshape(ROWT_DEV, nvt, edge, edge).transpose(0, 2, 1, 3).re...  12.1 us
  transfers between devices with their start and end apart: 6, of which 4 were waited for; matrix products, arithmetic and copies ran while one was open for 16% of the time, Pallas kernels for 0%

profile of v1, /device:TPU:1, one launch (start us, length us, event | category | flops | bytes accessed | tf_op | source)
XLA Modules:
  0.0 557.5 jit_solution(18403568870167409698)
XLA Ops:
  2.1 170.7 %collective-permute-done = bf16[992,3968]{1,0:T(8,128)(2,1)} collective-permute-done((bf16[992,3968]{1,0:T(8,128)(2,1)}, bf16[992,3968]{1,0:T(8,128)(2,1)}, u32[]{:S(2)}, u32[]{:S(2)}) %collective-permute-start) | collective-permute-done | bytes 7872544 | tf_op jit(solution)/shard_map/ppermute | solution.py:15
  181.6 9.8 %all-to-all-start = ((s32[32,16,1]{1,2,0:T(1,128)}), s32[32,16,1]{1,2,0:T(1,128)S(1)}, u32[]{:S(2)}, u32[]{:S(2)}) async-start(s32[32,16,1]{1,2,0:T(1,128)} %bitcast.2), calls=%async_computation | async-start | bytes 32768 | tf_op jit(solution)/shard_map/all_to_all | solution.py:48
  197.8 10.2 %scatter_custom_fusion.1 = bf16[512,4096]{1,0:T(8,128)(2,1)} fusion(s32[512]{0:T(512)S(1)} %get-tuple-element.6, bf16[512,4096]{1,0:T(8,128)(2,1)} %copy.20, bf16[]{:T(256)} %constant.103.clone.1), kind=kCustom, calls=%fused_computation.10 | custom fusion | bytes 4194816 | tf_op jit(solution)/shard_map/scatter | solution.py:41
  208.0 8.1 %all-to-all-start.1 = ((bf16[32,16,4096]{2,1,0:T(8,128)(2,1)}), bf16[32,16,4096]{2,1,0:T(8,128)(2,1)}, u32[]{:S(2)}, u32[]{:S(2)}) async-start(bf16[32,16,4096]{2,1,0:T(8,128)(2,1)} %bitcast.45), calls=%async_computation.1 | async-start | bytes 8388608 | tf_op jit(solution)/shard_map/all_to_all | solution.py:47
  217.4 50.6 %all-to-all-done.1 = bf16[32,16,4096]{2,1,0:T(8,128)(2,1)} async-done(((bf16[32,16,4096]{2,1,0:T(8,128)(2,1)}), bf16[32,16,4096]{2,1,0:T(8,128)(2,1)}, u32[]{:S(2)}, u32[]{:S(2)}) %all-to-all-start.1) | async-done | bytes 4194336 | tf_op jit(solution)/shard_map/all_to_all | solution.py:47
  268.0 10.4 %scatter_custom_fusion.2 = bf16[496,4096]{1,0:T(8,128)(2,1)} fusion(s32[512]{0:T(512)S(1)} %bitcast.51, bf16[512,4096]{1,0:T(8,128)(2,1)} %bitcast.7, bf16[]{:T(256)} %constant.103.clone.1), kind=kCustom, calls=%fused_computation.12 | custom fusion | bytes 4063744 | tf_op jit(solution)/shard_map/scatter | solution.py:51
  278.4 12.1 %reshape.91 = bf16[8,62,64,64]{3,2,1,0:T(8,128)(2,1)} reshape(bf16[496,4096]{1,0:T(8,128)(2,1)} %scatter_custom_fusion.2) | data formatting | bytes 8126464 | tf_op jit(solution)/shard_map/reshape | solution.py:54
  290.5 12.1 %copy.21 = bf16[8,64,62,64]{1,0,3,2:T(8,128)(2,1)} copy(bf16[8,64,62,64]{3,1,2,0:T(8,128)(2,1)} %bitcast.40) | data formatting | bytes 8126464 | tf_op jit(solution)/shard_map/transpose | solution.py:55
  302.5 11.5 %reshape.92 = bf16[512,3968]{0,1:T(8,128)(2,1)} reshape(bf16[8,64,62,64]{1,0,3,2:T(8,128)(2,1)} %copy.21) | data formatting | bytes 8126464 | tf_op jit(solution)/shard_map/reshape | solution.py:56
  314.0 29.9 %collective-permute-done.1 = bf16[992,3968]{1,0:T(8,128)(2,1)} collective-permute-done((bf16[992,3968]{1,0:T(8,128)(2,1)}, bf16[992,3968]{1,0:T(8,128)(2,1)}, u32[]{:S(2)}, u32[]{:S(2)}) %collective-permute-start.1) | collective-permute-done | bytes 7872544 | tf_op jit(solution)/shard_map/ppermute | solution.py:15
  344.0 7.0 %constant_dynamic-update-slice_fusion.7 = bf16[7936,3968]{1,0:T(8,128)(2,1)} fusion(bf16[992,3968]{1,0:T(8,128)(2,1)} %collective-permute-done.1), kind=kLoop, calls=%fused_computation.30 | loop fusion | bytes 15745024
  351.0 7.1 %constant_dynamic-update-slice_fusion.6 = bf16[7936,3968]{1,0:T(8,128)(2,1)} fusion(bf16[7936,3968]{1,0:T(8,128)(2,1)} %constant_dynamic-update-slice_fusion.7, bf16[992,3968]{1,0:T(8,128)(2,1)} %collective-permute-done), kind=kLoop, calls=%fused_computation.29 | loop fusion | bytes 15745024
  361.7 6.9 %constant_dynamic-update-slice_fusion.4 = bf16[7936,3968]{1,0:T(8,128)(2,1)} fusion(bf16[7936,3968]{1,0:T(8,128)(2,1)} %constant_dynamic-update-slice_fusion.5, bf16[992,3968]{1,0:T(8,128)(2,1)} %collective-permute-done.2), kind=kLoop, calls=%fused_computation.27 | loop fusion | bytes 15745024
  368.6 7.0 %constant_dynamic-update-slice_fusion.3 = bf16[7936,3968]{1,0:T(8,128)(2,1)} fusion(bf16[7936,3968]{1,0:T(8,128)(2,1)} %constant_dynamic-update-slice_fusion.4, bf16[992,3968]{1,0:T(8,128)(2,1)} %collective-permute-done.1), kind=kLoop, calls=%fused_computation.26 | loop fusion | bytes 15745024
  375.6 6.9 %constant_dynamic-update-slice_fusion.2 = bf16[7936,3968]{1,0:T(8,128)(2,1)} fusion(bf16[7936,3968]{1,0:T(8,128)(2,1)} %constant_dynamic-update-slice_fusion.3, bf16[992,3968]{1,0:T(8,128)(2,1)} %collective-permute-done), kind=kLoop, calls=%fused_computation.25 | loop fusion | bytes 15745024
  386.2 7.0 %constant_dynamic-update-slice_fusion = bf16[7936,3968]{1,0:T(8,128)(2,1)} fusion(bf16[7936,3968]{1,0:T(8,128)(2,1)} %constant_dynamic-update-slice_fusion.1, bf16[992,3968]{1,0:T(8,128)(2,1)} %collective-permute-done.2), kind=kLoop, calls=%fused_computation.23 | loop fusion | bytes 15745024 | tf_op jit(solution)/shard_map/jit(_roll_dynamic)/concatenate | solution.py:19
  393.2 22.9 %fusion.2 = bf16[512,3968]{1,0:T(8,128)(2,1)} fusion(bf16[512,3968]{0,1:T(8,128)(2,1)S(1)} %copy-done, bf16[7936,3968]{1,0:T(8,128)(2,1)} %constant_dynamic-update-slice_fusion, s32[]{:T(128)S(6)} %select_n.72), kind=kOutput, calls=%fused_computation.7 | convolution fusion | flops 16124936192 | bytes 39616516 | tf_op jit(solution)/shard_map/dot_general | solution.py:58
  422.5 10.9 %reshape.93 = bf16[8,64,62,64]{1,0,3,2:T(8,128)(2,1)} reshape(bf16[512,3968]{0,1:T(8,128)(2,1)} %copy.22) | data formatting | bytes 8126464 | tf_op jit(solution)/shard_map/reshape | solution.py:61
  433.4 11.9 %copy.23 = bf16[8,62,64,64]{3,2,1,0:T(8,128)(2,1)} copy(bf16[8,62,64,64]{2,0,3,1:T(8,128)(2,1)} %bitcast.41) | data formatting | bytes 8126464 | tf_op jit(solution)/shard_map/transpose | solution.py:62
  445.3 11.7 %reshape.94 = bf16[496,4096]{1,0:T(8,128)(2,1)} reshape(bf16[8,62,64,64]{3,2,1,0:T(8,128)(2,1)} %copy.23) | data formatting | bytes 8126464 | tf_op jit(solution)/shard_map/reshape | solution.py:63
  457.0 11.3 %gather_fusion = bf16[512,4096]{1,0:T(8,128)(2,1)} fusion(bf16[496,4096]{1,0:T(8,128)(2,1)} %reshape.94, s32[1024]{0:T(1024)S(1)} %pad_clamp_fusion.1), kind=kCustom, calls=%fused_computation | custom fusion | bytes 8390656 | tf_op jit(solution)/shard_map/jit(_take)/gather | solution.py:65
  472.8 10.1 %all-to-all-start.2 = ((bf16[32,16,4096]{2,1,0:T(8,128)(2,1)}), bf16[32,16,4096]{2,1,0:T(8,128)(2,1)}, u32[]{:S(2)}, u32[]{:S(2)}) async-start(bf16[32,16,4096]{2,1,0:T(8,128)(2,1)} %broadcast_select_fusion), calls=%async_computation.2 | async-start | bytes 8388608 | tf_op jit(solution)/shard_map/all_to_all | solution.py:66
  482.9 52.1 %all-to-all-done.2 = bf16[32,16,4096]{2,1,0:T(8,128)(2,1)} async-done(((bf16[32,16,4096]{2,1,0:T(8,128)(2,1)}), bf16[32,16,4096]{2,1,0:T(8,128)(2,1)}, u32[]{:S(2)}, u32[]{:S(2)}) %all-to-all-start.2) | async-done | bytes 4194336 | tf_op jit(solution)/shard_map/all_to_all | solution.py:66
  535.0 11.3 %gather_fusion.1 = bf16[512,4096]{1,0:T(8,128)(2,1)} fusion(bf16[512,4096]{1,0:T(8,128)(2,1)} %bitcast.11, s32[1024]{0:T(1024)S(1)} %pad_clamp_fusion), kind=kCustom, calls=%fused_computation.1 | custom fusion | bytes 8390656 | tf_op jit(solution)/shard_map/jit(_take)/gather | solution.py:67
  (36 shorter events, 47.8 us)
Async XLA Ops:
  0.0 172.9 %collective-permute-start = (bf16[992,3968]{1,0:T(8,128)(2,1)}, bf16[992,3968]{1,0:T(8,128)(2,1)}, u32[]{:S(2)}, u32[]{:S(2)}) collective-permute-start(bf16[992,3968]{1,0:T(8,128)(2,1)} %param.7), channel_id=1, source_target_pairs={{0,32},{32,64},{64,96},{96,0},{1,33},{33,65},{65,97},{97,1},{2,34}... | collective-permute-start | bytes 23617544 | tf_op jit(solution)/shard_map/ppermute | solution.py:15
  172.9 171.1 %collective-permute-start.1 = (bf16[992,3968]{1,0:T(8,128)(2,1)}, bf16[992,3968]{1,0:T(8,128)(2,1)}, u32[]{:S(2)}, u32[]{:S(2)}) collective-permute-start(bf16[992,3968]{1,0:T(8,128)(2,1)} %collective-permute-done), channel_id=1, source_target_pairs={{0,32},{32,64},{64,96},{96,0},{1,33},{33,65},{65,97},{97,1},{2,34}... | collective-permute-start | bytes 23617544 | tf_op jit(solution)/shard_map/ppermute | solution.py:15
  172.9 188.8 %collective-permute-start.2 = (bf16[992,3968]{1,0:T(8,128)(2,1)}, bf16[992,3968]{1,0:T(8,128)(2,1)}, u32[]{:S(2)}, u32[]{:S(2)}) collective-permute-start(bf16[992,3968]{1,0:T(8,128)(2,1)} %param.7), channel_id=1, source_target_pairs={{0,96},{32,0},{64,32},{96,64},{1,97},{33,1},{65,33},{97,65},{2,98}... | collective-permute-start | bytes 23617544 | tf_op jit(solution)/shard_map/ppermute | solution.py:17
  181.6 26.4 %all-to-all-start = ((s32[32,16,1]{1,2,0:T(1,128)}), s32[32,16,1]{1,2,0:T(1,128)S(1)}, u32[]{:S(2)}, u32[]{:S(2)}) async-start(s32[32,16,1]{1,2,0:T(1,128)} %bitcast.2), calls=%async_computation | async-start | bytes 32768 | tf_op jit(solution)/shard_map/all_to_all | solution.py:48
  208.0 60.0 %all-to-all-start.1 = ((bf16[32,16,4096]{2,1,0:T(8,128)(2,1)}), bf16[32,16,4096]{2,1,0:T(8,128)(2,1)}, u32[]{:S(2)}, u32[]{:S(2)}) async-start(bf16[32,16,4096]{2,1,0:T(8,128)(2,1)} %bitcast.45), calls=%async_computation.1 | async-start | bytes 8388608 | tf_op jit(solution)/shard_map/all_to_all | solution.py:47
  344.0 14.1 %slice-start = ((s8[7872512]{0:T(1024)(128)(4,1)}), s8[4194304]{0:T(1024)(128)(4,1)S(1)}, s32[]{:S(2)}) async-start(s8[7872512]{0:T(1024)(128)(4,1)} %bitcast.42), calls=%async_computation.3 | async-start | bytes 8388608
  351.0 7.1 %slice-start.1 = ((s8[7872512]{0:T(1024)(128)(4,1)}), s8[3678208]{0:T(1024)(128)(4,1)S(1)}, s32[]{:S(2)}) async-start(s8[7872512]{0:T(1024)(128)(4,1)} %bitcast.42), calls=%async_computation.4 | async-start | bytes 7356416
  386.2 7.0 %copy-start = (bf16[512,3968]{0,1:T(8,128)(2,1)S(1)}, bf16[512,3968]{0,1:T(8,128)(2,1)}, u32[]{:S(2)}) copy-start(bf16[512,3968]{0,1:T(8,128)(2,1)} %reshape.92) | copy-start | bytes 12189700
  472.8 62.2 %all-to-all-start.2 = ((bf16[32,16,4096]{2,1,0:T(8,128)(2,1)}), bf16[32,16,4096]{2,1,0:T(8,128)(2,1)}, u32[]{:S(2)}, u32[]{:S(2)}) async-start(bf16[32,16,4096]{2,1,0:T(8,128)(2,1)} %broadcast_select_fusion), calls=%async_computation.2 | async-start | bytes 8388608 | tf_op jit(solution)/shard_map/all_to_all | solution.py:66
